TPU v7x, 512 devices: a whole 4x8x8 slice. The times are simulated.
512 devices in a mesh: section: 32 (over z, x), et: 16 (over y, core).
Axes of the slice: x: 4, y: 8, z: 8, core: 2. Of those that a mesh axis runs over, the one named last changes fastest.
Arguments:
- x_fwd: bfloat16 [32, 256, 3072], P('section', 'et'), may hold values from -6 to 6
- act_fwd: bfloat16 [32, 256, 8192], P('section', None, 'et'), may hold values from -6 to 6
- ids_fwd: int32 [32, 256, 2], P('section'), may hold values from 0 to 7, as said below
- x_bwd: bfloat16 [32, 256, 3072], P('section', 'et'), may hold values from -6 to 6
- act_bwd: bfloat16 [32, 256, 8192], P('section', None, 'et'), may hold values from -6 to 6
- ids_bwd: int32 [32, 256, 2], P('section'), may hold values from 0 to 7, as said below
- grad_out: bfloat16 [32, 256, 3072], P('section', 'et'), may hold values from -6 to 6
- gain: bfloat16 [32, 3072], P('section'), may hold values from 0.099609375 to 1.8984375
- w_router: bfloat16 [32, 3072, 8], P('section'), may hold values from -0.21875 to 0.21875
- w_down: bfloat16 [32, 8192, 3072], P('section', 'et'), may hold values from -0.0625 to 0.0625
Outputs:
- fwd_in: bfloat16 [32, 256, 3072], P('section', 'et')
- incoming_gradient: bfloat16 [32, 256, 3072], P('section', 'et')
- dact: bfloat16 [32, 256, 8192], P('section', None, 'et')
Inputs may be any that keep to these rules, and one draw needn't show every extreme that they name: `ids_fwd`: each token names 2 different experts; in each section's micro-batch exactly 128 tokens name expert 0. `ids_bwd`: each token names 2 different experts; in each section's micro-batch exactly 128 tokens name expert 0.
All inputs are finite; a program needn't handle non-finite values.
Results may differ from a plain program's by a relative error of at most 0.014.
Values may be sent and summed in bfloat16 or wider, within the bound.
No kernel may reach another device: no remote copies, remote signals or barrier semaphores. Data moves between devices by JAX's collectives and lax.ppermute only.
A program may use at most 64 MiB of HBM per device.

v0:
```python
import jax
import jax.numpy as jnp
from jax import lax
from jax.sharding import PartitionSpec as P


def from_behind(value, axis, steps):
    count = lax.axis_size(axis)
    first, last = (max(0, -steps), min(count, count - steps))
    return lax.ppermute(value, axis, [(source, source + steps) for source in range(first, last)])


def norm_logits(inputs, gain, w_router):
    wide = inputs.astype(jnp.float32)
    inverse = lax.rsqrt(jnp.mean(wide * wide, axis=-1, keepdims=True) + 1e-05)
    normed = (wide * inverse * gain.astype(jnp.float32)).astype(jnp.bfloat16)
    logits = jnp.dot(normed, w_router, preferred_element_type=jnp.float32).astype(jnp.bfloat16)
    return (wide, inverse, logits)


def routing(logits, chosen, experts):
    route = jnp.sum((chosen == 0).astype(jnp.float32), axis=1)
    partner = jnp.minimum(jnp.sum(chosen, axis=1), experts - 1)
    labels = jnp.arange(experts, dtype=jnp.int32)
    onehot = (partner[:, None] == labels[None, :]).astype(jnp.float32)
    wide_logits = logits.astype(jnp.float32)
    sigma = jax.nn.sigmoid(wide_logits[:, 0] - jnp.sum(wide_logits * onehot, axis=1))
    return (route, onehot, sigma, route * sigma)


def arrange(chosen):
    member = jnp.sum((chosen == 0).astype(jnp.int32), axis=1)
    tally = jnp.sum(member)
    before = jnp.cumsum(member) - member
    after = jnp.cumsum(1 - member) - (1 - member)
    place = jnp.where(member == 1, before, tally + after)
    ordering = jnp.zeros_like(member).at[place].set(jnp.arange(member.shape[0], dtype=jnp.int32))
    return (member, place, ordering)


def spread_back(compact, member, place, capacity):
    safe = jnp.minimum(place, capacity - 1)
    return jnp.where(member[:, None] == 1, compact[safe], 0.0)


def shards(x_fwd, act_fwd, ids_fwd, x_bwd, act_bwd, ids_bwd, grad_out, gain, w_router, w_down):
    x_fwd, act_fwd, ids_fwd, x_bwd, act_bwd = (
        x_fwd[0],
        act_fwd[0],
        ids_fwd[0],
        x_bwd[0],
        act_bwd[0],
    )
    ids_bwd, grad_out, gain, w_router, w_down = (
        ids_bwd[0],
        grad_out[0],
        gain[0],
        w_router[0],
        w_down[0],
    )
    experts = w_router.shape[1]
    tokens = ids_fwd.shape[0]
    capacity = tokens // 2
    own_rows = x_fwd.shape[0]
    first_row = lax.axis_index("et") * own_rows
    wide_f, inverse_f, logit_f = norm_logits(x_fwd, gain, w_router)
    backward_wide_rows, backward_inverse_norm, logit_b = norm_logits(x_bwd, gain, w_router)
    full_f, full_b, full_g = (
        lax.all_gather(logit_f, "et", axis=0, tiled=True),
        lax.all_gather(logit_b, "et", axis=0, tiled=True),
        lax.all_gather(grad_out, "et", axis=0, tiled=True),
    )
    route_f, onehot_f, sigma_f, coef_f = routing(full_f, ids_fwd, experts)
    member_f, place_f, order_f = arrange(ids_fwd)
    chosen_f = order_f[:capacity]
    compact = (
        jnp.dot(act_fwd[chosen_f], w_down, preferred_element_type=jnp.float32)
        * coef_f[chosen_f][:, None]
    )
    summed = lax.psum(compact.astype(jnp.bfloat16), "et").astype(jnp.float32)
    member_own = lax.dynamic_slice_in_dim(member_f, first_row, own_rows, 0)
    place_own = lax.dynamic_slice_in_dim(place_f, first_row, own_rows, 0)
    y_mine = spread_back(summed, member_own, place_own, capacity)
    layer_out = (wide_f + y_mine).astype(jnp.bfloat16)
    route_b, onehot_b, sigma_b, backward_coefficient = routing(full_b, ids_bwd, experts)
    member_b, place_b, order_b = arrange(ids_bwd)
    chosen_b = order_b[:capacity]
    up_compact = lax.dot_general(
        full_g[chosen_b], w_down, (((1,), (1,)), ((), ())), preferred_element_type=jnp.float32
    )
    back_up = spread_back(up_compact, member_b, place_b, capacity)
    dact = (backward_coefficient[:, None] * back_up).astype(jnp.bfloat16)
    dprob_part = jnp.sum(act_bwd.astype(jnp.float32) * back_up, axis=1)
    dprob_all = lax.psum(dprob_part, "et")
    dprob_mine = lax.dynamic_slice_in_dim(dprob_all, first_row, own_rows, 0)
    route_mine = lax.dynamic_slice_in_dim(route_b, first_row, own_rows, 0)
    sigma_mine = lax.dynamic_slice_in_dim(sigma_b, first_row, own_rows, 0)
    onehot_mine = lax.dynamic_slice_in_dim(onehot_b, first_row, own_rows, 0)
    slope = route_mine * dprob_mine * sigma_mine * (1.0 - sigma_mine)
    router_wide = w_router.astype(jnp.float32)
    spread = router_wide[:, 0][None, :] - jnp.dot(
        onehot_mine, router_wide.T, precision=lax.Precision.HIGHEST
    )
    dnormed = slope[:, None] * spread
    scaled_rows = dnormed * gain.astype(jnp.float32)
    normalized_input = backward_wide_rows * backward_inverse_norm
    norm_input_gradient = backward_inverse_norm * (
        scaled_rows
        - normalized_input * jnp.mean(scaled_rows * normalized_input, axis=-1, keepdims=True)
    )
    input_grad = (grad_out.astype(jnp.float32) + norm_input_gradient).astype(jnp.bfloat16)
    fwd_in = from_behind(layer_out, "section", 1)
    incoming_gradient = from_behind(input_grad, "section", -1)
    return (fwd_in[None], incoming_gradient[None], dact[None])


def solution(mesh):
    placed = (
        P("section", "et", None),
        P("section", None, "et"),
        P("section", None, None),
        P("section", "et", None),
        P("section", None, "et"),
        P("section", None, None),
        P("section", "et", None),
        P("section", None),
        P("section", None, None),
        P("section", "et", None),
    )
    return jax.shard_map(
        shards,
        mesh=mesh,
        in_specs=placed,
        out_specs=(P("section", "et", None), P("section", "et", None), P("section", None, "et")),
        check_vma=False,
    )
```

profile of v0, /device:TPU:6, one launch (start us, length us, event | category | flops | bytes accessed | tf_op | source)
XLA Modules:
  0.0 256.7 jit_solution(1746351903962819599)
XLA Ops:
  7.2 0.9 convert_reduce_fusion.5
  8.1 1.4 convert_reduce_fusion
  11.9 1.4 scatter_custom_fusion
  14.1 1.0 fusion.22
  15.1 1.1 fusion.6
  16.3 17.6 %all-gather.1 = bf16[16,16,8]{1,2,0:T(8,128)(2,1)S(1)} all-gather(bf16[1,16,8]{1,2,0:T(8,128)(2,1)S(1)} %fusion.6), channel_id=1, replica_groups=mesh['section'=32,'et'=16] {'et'}, dimensions={0}, use_global_device_ids=true | all-gather | bytes 4352 | tf_op jit(solution)/shard_map/all_gather | solution.py:69
  34.1 1.9 gather_fusion
  36.0 1.3 gather_fusion.1
  37.3 1.5 fusion
  40.4 1.0 fusion.7
  42.6 1.2 compare_select_fusion
  43.8 1.4 scatter_custom_fusion.1
  45.9 15.0 %all-gather.2 = bf16[16,16,8]{1,2,0:T(8,128)(2,1)S(1)} all-gather(bf16[1,16,8]{1,2,0:T(8,128)(2,1)S(1)} %fusion.7), channel_id=1, replica_groups=mesh['section'=32,'et'=16] {'et'}, dimensions={0}, use_global_device_ids=true | all-gather | bytes 4352 | tf_op jit(solution)/shard_map/all_gather | solution.py:70
  63.9 1.4 slice_convert_fusion
  65.3 92.2 %all-reduce.2.cloned.1.call-done = bf16[128,3072]{1,0:T(8,128)(2,1)} async-done(((bf16[128,3072]{1,0:T(8,128)(2,1)}), bf16[128,3072]{1,0:T(8,128)(2,1)}) %all-reduce.2.cloned.1.call-update) | async-done | bytes 786448 | tf_op jit(solution)/shard_map/psum | solution.py:80
  157.6 2.4 convert_element_type.106
  160.0 2.2 gather_fusion.2
  162.2 0.8 fusion.23
  163.0 3.5 %collective-permute-start = (bf16[16,3072]{1,0:T(8,128)(2,1)S(1)}, bf16[16,3072]{1,0:T(8,128)(2,1)}, u32[]{:S(2)}, u32[]{:S(2)}) collective-permute-start(bf16[16,3072]{1,0:T(8,128)(2,1)S(1)} %fusion.23), channel_id=1, source_target_pairs={{0,16},{16,32},{32,48},{48,64},{64,80},{80,96},{96,112},{112,128},... | collective-permute-start | bytes 294920 | tf_op jit(solution)/shard_map/ppermute | solution.py:10
  167.2 2.4 collective-permute-done
  169.6 32.3 %all-gather.5.cloned.1.call-done = bf16[1,256,3072]{2,1,0:T(8,128)(2,1)} async-done(((bf16[1,16,3072]{2,1,0:T(8,128)(2,1)}), bf16[1,256,3072]{2,1,0:T(8,128)(2,1)}) %all-gather.5.cloned.1.call-update) | async-done | bytes 1572880 | tf_op jit(solution)/shard_map/all_gather | solution.py:71
  201.9 4.5 %gather_fusion.3 = bf16[128,3072]{1,0:T(8,128)(2,1)} fusion(bf16[256,3072]{1,0:T(8,128)(2,1)} %bitcast.108, s32[1024]{0:T(1024)} %pad_clamp_fusion.1), kind=kCustom, calls=%fused_computation.3 | custom fusion | bytes 1573376 | tf_op jit(solution)/shard_map/gather | solution.py:89
  206.3 2.3 fusion.3
  208.7 1.8 gather_fusion.4
  210.5 1.3 fusion.8
  211.8 24.9 %psum.15 = f32[256]{0:T(256)S(1)} all-reduce(f32[256]{0:T(256)S(1)} %fusion.8), channel_id=1, replica_groups=mesh['section'=32,'et'=16] {'et'}, use_global_device_ids=true, to_apply=%region_22.23 | all-reduce | flops 256 | bytes 2048 | tf_op jit(solution)/shard_map/psum | solution.py:94
  236.8 1.2 fusion.17
  238.0 1.0 fusion.21
  239.0 2.8 %collective-permute-start.1 = (bf16[16,3072]{1,0:T(8,128)(2,1)S(1)}, bf16[16,3072]{1,0:T(8,128)(2,1)S(1)}, u32[]{:S(2)}, u32[]{:S(2)}) collective-permute-start(bf16[16,3072]{1,0:T(8,128)(2,1)S(1)} %fusion.21), channel_id=1, source_target_pairs={{16,0},{32,16},{48,32},{64,48},{80,64},{96,80},{112,96},{128,112},... | collective-permute-start | bytes 294920 | tf_op jit(solution)/shard_map/ppermute | solution.py:10
  241.8 1.9 fusion.10
  243.7 4.0 %collective-permute-done.1 = bf16[16,3072]{1,0:T(8,128)(2,1)S(1)} collective-permute-done((bf16[16,3072]{1,0:T(8,128)(2,1)S(1)}, bf16[16,3072]{1,0:T(8,128)(2,1)S(1)}, u32[]{:S(2)}, u32[]{:S(2)}) %collective-permute-start.1) | collective-permute-done | bytes 98336 | tf_op jit(solution)/shard_map/ppermute | solution.py:10
  247.6 1.5 copy.20
  (79 shorter events, 11.3 us)
Async XLA Ops:
  7.2 30.1 %copy-start = (bf16[1,512,3072]{2,1,0:T(8,128)(2,1)S(1)}, bf16[1,512,3072]{2,1,0:T(8,128)(2,1)}, u32[]{:S(2)}) copy-start(bf16[1,512,3072]{2,1,0:T(8,128)(2,1)} %param.19) | copy-start | bytes 9437188
  7.2 150.4 %all-reduce.2.cloned.1.call-start = ((), (), s32[]{:S(2)}) async-start(), calls=%async_computation | async-start | bytes 1572864 | tf_op jit(solution)/shard_map/psum | solution.py:80
  34.0 6.2 %copy-start.2 = (bf16[1,16,3072]{2,1,0:T(8,128)(2,1)S(1)}, bf16[1,16,3072]{2,1,0:T(8,128)(2,1)}, u32[]{:S(2)}) copy-start(bf16[1,16,3072]{2,1,0:T(8,128)(2,1)} %param.13) | copy-start | bytes 294916
  35.9 25.7 %copy-start.4 = (s32[1,256,2]{1,2,0:T(2,128)S(1)}, s32[1,256,2]{1,2,0:T(2,128)}, u32[]{:S(2)}) copy-start(s32[1,256,2]{1,2,0:T(2,128)} %param.15) | copy-start | bytes 6148
  38.8 123.5 %copy-start.1 = (bf16[1,16,3072]{2,1,0:T(8,128)(2,1)S(1)}, bf16[1,16,3072]{2,1,0:T(8,128)(2,1)}, u32[]{:S(2)}) copy-start(bf16[1,16,3072]{2,1,0:T(8,128)(2,1)} %param.10) | copy-start | bytes 294916
  38.8 163.1 %all-gather.5.cloned.1.call-start = ((), (), s32[]{:S(2)}) async-start(), calls=%async_computation.1 | async-start | bytes 1671168 | tf_op jit(solution)/shard_map/all_gather | solution.py:71
  40.4 1.0 copy-start.9
  163.0 6.6 %collective-permute-start = (bf16[16,3072]{1,0:T(8,128)(2,1)S(1)}, bf16[16,3072]{1,0:T(8,128)(2,1)}, u32[]{:S(2)}, u32[]{:S(2)}) collective-permute-start(bf16[16,3072]{1,0:T(8,128)(2,1)S(1)} %fusion.23), channel_id=1, source_target_pairs={{0,16},{16,32},{32,48},{48,64},{64,80},{80,96},{96,112},{112,128},... | collective-permute-start | bytes 294920 | tf_op jit(solution)/shard_map/ppermute | solution.py:10
  208.7 1.8 copy-start.8
  208.7 28.0 %copy-start.6 = (f32[256]{0:T(256)S(1)}, f32[256]{0:T(256)}, u32[]{:S(2)}) copy-start(f32[256]{0:T(256)} %add_divide_fusion) | copy-start | bytes 3076
  208.7 28.1 %copy-start.3 = (f32[3072,1]{0,1:T(1,128)S(1)}, f32[3072,1]{0,1:T(1,128)}, u32[]{:S(2)}) copy-start(f32[3072,1]{0,1:T(1,128)} %slice_convert_fusion) | copy-start | bytes 36868
  208.7 28.1 %copy-start.7 = (pred[256,8]{0,1:T(8,128)(4,1)S(1)}, pred[256,8]{0,1:T(8,128)(4,1)}, u32[]{:S(2)}) copy-start(pred[256,8]{0,1:T(8,128)(4,1)} %iota_compare_fusion) | copy-start | bytes 6148
  208.7 33.1 %copy-start.5 = (f32[256,1]{0,1:T(1,128)S(1)}, f32[256,1]{0,1:T(1,128)}, u32[]{:S(2)}) copy-start(f32[256,1]{0,1:T(1,128)} %get-tuple-element.14) | copy-start | bytes 3076
  239.0 8.6 %collective-permute-start.1 = (bf16[16,3072]{1,0:T(8,128)(2,1)S(1)}, bf16[16,3072]{1,0:T(8,128)(2,1)S(1)}, u32[]{:S(2)}, u32[]{:S(2)}) collective-permute-start(bf16[16,3072]{1,0:T(8,128)(2,1)S(1)} %fusion.21), channel_id=1, source_target_pairs={{16,0},{32,16},{48,32},{64,48},{80,64},{96,80},{112,96},{128,112},... | collective-permute-start | bytes 294920 | tf_op jit(solution)/shard_map/ppermute | solution.py:10
Sparse Core Ops, SparseCore 0:
  38.9 118.5 all-reduce.1
  159.7 42.1 all-gather.4
where the time goes:
time: 257 us
  waiting for transfers between devices  132 us (51%)
  blocking collectives  57.5 us (22%)
  other arithmetic  22.1 us (9%)
  local copies, waits for them, and re-layouts  17.6 us (7%)
  between operations  14.3 us (6%)
  matrix products  7.15 us (3%)
  starting transfers between devices  6.38 us (2%)
    psum x1, waiting for transfers between devices, shards(): summed = lax.psum(compact.astype(jnp.bfloat16), 'et').astype(jnp.float32)  92.2 us
    all_gather x1, waiting for transfers between devices, shards(): lax.all_gather(grad_out, 'et', axis=0, tiled=True)  32.3 us
    psum x1, blocking collectives, shards(): dprob_all = lax.psum(dprob_part, 'et')  24.9 us
    all_gather x1, blocking collectives, shards(): lax.all_gather(logit_f, 'et', axis=0, tiled=True)  17.6 us
    all_gather x1, blocking collectives, shards(): lax.all_gather(logit_b, 'et', axis=0, tiled=True)  15 us
    ppermute x2, waiting for transfers between devices, from_behind(): lax.ppermute(value, axis, [(source, source + steps) for source in range(f...  6.38 us
    ppermute x2, starting transfers between devices, from_behind(): lax.ppermute(value, axis, [(source, source + steps) for source in range(f...  6.3 us
  transfers between devices with their start and end apart: 4, of which 4 were waited for; matrix products, arithmetic and copies ran while one was open for 7% of the time, Pallas kernels for 0%

commit v1 on v0

--- a/solution.py
+++ b/solution.py
@@ -2,6 +2,19 @@
 import jax.numpy as jnp
 from jax import lax
 from jax.sharding import PartitionSpec as P
+
+
+def collect(x, axis, dim):
+    ways = lax.axis_size(axis)
+    up = [(d, (d + 1) % ways) for d in range(ways)]
+    down = [(d, (d - 1) % ways) for d in range(ways)]
+    earlier, later = ([x], [x])
+    for _ in range(ways // 2):
+        earlier.append(lax.ppermute(earlier[-1], axis, up))
+    for _ in range((ways - 1) // 2):
+        later.append(lax.ppermute(later[-1], axis, down))
+    line = jnp.concatenate([*earlier[::-1], *later[1:]], axis=dim)
+    return jnp.roll(line, (lax.axis_index(axis) - ways // 2) * x.shape[dim], axis=dim)
 
 
 def from_behind(value, axis, steps):
@@ -67,7 +80,7 @@
     backward_wide_rows, backward_inverse_norm, logit_b = norm_logits(x_bwd, gain, w_router)
     full_f, full_b, full_g = (
         lax.all_gather(logit_f, "et", axis=0, tiled=True),
-        lax.all_gather(logit_b, "et", axis=0, tiled=True),
+        collect(logit_b, "et", 0),
         lax.all_gather(grad_out, "et", axis=0, tiled=True),
     )
     route_f, onehot_f, sigma_f, coef_f = routing(full_f, ids_fwd, experts)

time: 257 us -> 258 us (level)
  starting transfers between devices: 6.38 us -> 26.9 us
  blocking collectives: 57.5 us -> 42.6 us
  waiting for transfers between devices: 132 us -> 126 us
    ppermute x0 -> x15, starting transfers between devices: none -> 20.5 us  [the longest x7 20.1 us: collect(): later.append(lax.ppermute(later[-1], axis, down))]
    psum x1, waiting for transfers between devices: 92.2 us -> 76.4 us  [shards(): summed = lax.psum(compact.astype(jnp.bfloat16), 'et').astype(jnp.float32)]
    all_gather x1 -> x0, blocking collectives: 15 us -> none  [shards(): lax.all_gather(logit_b, 'et', axis=0, tiled=True)]
    ppermute x0 -> x15, waiting for transfers between devices: none -> 11.4 us  [the longest x8 7.29 us: collect(): earlier.append(lax.ppermute(earlier[-1], axis, up))]
  transfers between devices with their start and end apart: 4 -> 19, of which waited for: 4 -> 17; matrix products, arithmetic and copies ran while one was open for 7% -> 7% of each run, Pallas kernels for 0% -> 0%
where the time goes in v1:
time: 258 us; the launch traced here: 257 us
  waiting for transfers between devices  126 us (49%)
  blocking collectives  42.6 us (17%)
  starting transfers between devices  26.9 us (10%)
  other arithmetic  21.7 us (8%)
  local copies, waits for them, and re-layouts  17.7 us (7%)
  between operations  14.4 us (6%)
  matrix products  7.15 us (3%)
    psum x1, waiting for transfers between devices, shards(): summed = lax.psum(compact.astype(jnp.bfloat16), 'et').astype(jnp.float32)  76.4 us
    all_gather x1, waiting for transfers between devices, shards(): lax.all_gather(grad_out, 'et', axis=0, tiled=True)  32.3 us
    psum x1, blocking collectives, shards(): dprob_all = lax.psum(dprob_part, 'et')  24.9 us
    ppermute x7, starting transfers between devices, collect(): later.append(lax.ppermute(later[-1], axis, down))  20.1 us
    all_gather x1, blocking collectives, shards(): lax.all_gather(logit_f, 'et', axis=0, tiled=True)  17.6 us
    ppermute x8, waiting for transfers between devices, collect(): earlier.append(lax.ppermute(earlier[-1], axis, up))  7.29 us
    ppermute x2, waiting for transfers between devices, from_behind(): lax.ppermute(value, axis, [(source, source + steps) for source in range(f...  6.39 us
    ppermute x2, starting transfers between devices, from_behind(): lax.ppermute(value, axis, [(source, source + steps) for source in range(f...  6.3 us
  transfers between devices with their start and end apart: 19, of which 17 were waited for; matrix products, arithmetic and copies ran while one was open for 7% of the time, Pallas kernels for 0%

profile of v1, /device:TPU:6, one launch (start us, length us, event | category | flops | bytes accessed | tf_op | source)
XLA Modules:
  0.0 256.8 jit_solution(5038064221802888046)
XLA Ops:
  8.1 1.4 convert_reduce_fusion
  11.9 1.4 scatter_custom_fusion
  16.3 17.6 %all-gather.1 = bf16[16,16,8]{1,2,0:T(8,128)(2,1)S(1)} all-gather(bf16[1,16,8]{1,2,0:T(8,128)(2,1)S(1)} %fusion.6), channel_id=1, replica_groups=mesh['section'=32,'et'=16] {'et'}, dimensions={0}, use_global_device_ids=true | all-gather | bytes 4352 | tf_op jit(solution)/shard_map/all_gather | solution.py:82
  34.1 1.9 gather_fusion
  36.0 1.3 gather_fusion.1
  37.3 1.5 fusion
  40.4 2.6 %collective-permute-start.9 = (bf16[16,8]{0,1:T(8,128)(2,1)S(1)}, bf16[16,8]{0,1:T(8,128)(2,1)S(1)}, u32[]{:S(2)}, u32[]{:S(2)}) collective-permute-start(bf16[16,8]{0,1:T(8,128)(2,1)S(1)} %convolution_convert_fusion), channel_id=1, source_target_pairs={{0,15},{1,0},{2,1},{3,2},{4,3},{5,4},{6,5},{7,6},{8,7},{9,8},{10,9... | collective-permute-start | bytes 776 | tf_op jit(solution)/shard_map/ppermute | solution.py:15
  45.6 1.4 scatter_custom_fusion.1
  48.8 1.4 slice_convert_fusion
  51.4 3.0 %collective-permute-start.10 = (bf16[16,8]{0,1:T(8,128)(2,1)S(1)}, bf16[16,8]{0,1:T(8,128)(2,1)S(1)}, u32[]{:S(2)}, u32[]{:S(2)}) collective-permute-start(bf16[16,8]{0,1:T(8,128)(2,1)S(1)} %collective-permute-done.9), channel_id=1, source_target_pairs={{0,15},{1,0},{2,1},{3,2},{4,3},{5,4},{6,5},{7,6},{8,7},{9,8},{10,9... | collective-permute-start | bytes 776 | tf_op jit(solution)/shard_map/ppermute | solution.py:15
  55.7 2.9 %collective-permute-start.11 = (bf16[16,8]{0,1:T(8,128)(2,1)S(1)}, bf16[16,8]{0,1:T(8,128)(2,1)S(1)}, u32[]{:S(2)}, u32[]{:S(2)}) collective-permute-start(bf16[16,8]{0,1:T(8,128)(2,1)S(1)} %collective-permute-done.10), channel_id=1, source_target_pairs={{0,15},{1,0},{2,1},{3,2},{4,3},{5,4},{6,5},{7,6},{8,7},{9,8},{10,9... | collective-permute-start | bytes 776 | tf_op jit(solution)/shard_map/ppermute | solution.py:15
  59.9 2.9 %collective-permute-start.12 = (bf16[16,8]{0,1:T(8,128)(2,1)S(1)}, bf16[16,8]{0,1:T(8,128)(2,1)S(1)}, u32[]{:S(2)}, u32[]{:S(2)}) collective-permute-start(bf16[16,8]{0,1:T(8,128)(2,1)S(1)} %collective-permute-done.11), channel_id=1, source_target_pairs={{0,15},{1,0},{2,1},{3,2},{4,3},{5,4},{6,5},{7,6},{8,7},{9,8},{10,9... | collective-permute-start | bytes 776 | tf_op jit(solution)/shard_map/ppermute | solution.py:15
  64.1 2.9 %collective-permute-start.13 = (bf16[16,8]{0,1:T(8,128)(2,1)S(1)}, bf16[16,8]{0,1:T(8,128)(2,1)S(1)}, u32[]{:S(2)}, u32[]{:S(2)}) collective-permute-start(bf16[16,8]{0,1:T(8,128)(2,1)S(1)} %collective-permute-done.12), channel_id=1, source_target_pairs={{0,15},{1,0},{2,1},{3,2},{4,3},{5,4},{6,5},{7,6},{8,7},{9,8},{10,9... | collective-permute-start | bytes 776 | tf_op jit(solution)/shard_map/ppermute | solution.py:15
  68.4 2.9 %collective-permute-start.14 = (bf16[16,8]{0,1:T(8,128)(2,1)S(1)}, bf16[16,8]{0,1:T(8,128)(2,1)S(1)}, u32[]{:S(2)}, u32[]{:S(2)}) collective-permute-start(bf16[16,8]{0,1:T(8,128)(2,1)S(1)} %collective-permute-done.13), channel_id=1, source_target_pairs={{0,15},{1,0},{2,1},{3,2},{4,3},{5,4},{6,5},{7,6},{8,7},{9,8},{10,9... | collective-permute-start | bytes 776 | tf_op jit(solution)/shard_map/ppermute | solution.py:15
  72.6 2.9 %collective-permute-start.15 = (bf16[16,8]{0,1:T(8,128)(2,1)S(1)}, bf16[16,8]{0,1:T(8,128)(2,1)S(1)}, u32[]{:S(2)}, u32[]{:S(2)}) collective-permute-start(bf16[16,8]{0,1:T(8,128)(2,1)S(1)} %collective-permute-done.14), channel_id=1, source_target_pairs={{0,15},{1,0},{2,1},{3,2},{4,3},{5,4},{6,5},{7,6},{8,7},{9,8},{10,9... | collective-permute-start | bytes 776 | tf_op jit(solution)/shard_map/ppermute | solution.py:15
  76.8 3.5 %collective-permute-done.8 = bf16[16,8]{0,1:T(8,128)(2,1)S(1)} collective-permute-done((bf16[16,8]{0,1:T(8,128)(2,1)S(1)}, bf16[16,8]{0,1:T(8,128)(2,1)S(1)}, u32[]{:S(2)}, u32[]{:S(2)}) %collective-permute-start.8) | collective-permute-done | bytes 288 | tf_op jit(solution)/shard_map/ppermute | solution.py:13
  81.2 76.4 %all-reduce.2.cloned.1.call-done = bf16[128,3072]{1,0:T(8,128)(2,1)} async-done(((bf16[128,3072]{1,0:T(8,128)(2,1)}), bf16[128,3072]{1,0:T(8,128)(2,1)}) %all-reduce.2.cloned.1.call-update) | async-done | bytes 786448 | tf_op jit(solution)/shard_map/psum | solution.py:93
  157.6 2.4 convert_element_type.106
  160.0 2.2 gather_fusion.2
  163.0 3.5 %collective-permute-start = (bf16[16,3072]{1,0:T(8,128)(2,1)S(1)}, bf16[16,3072]{1,0:T(8,128)(2,1)}, u32[]{:S(2)}, u32[]{:S(2)}) collective-permute-start(bf16[16,3072]{1,0:T(8,128)(2,1)S(1)} %fusion.22), channel_id=1, source_target_pairs={{0,16},{16,32},{32,48},{48,64},{64,80},{80,96},{96,112},{112,128},... | collective-permute-start | bytes 294920 | tf_op jit(solution)/shard_map/ppermute | solution.py:23
  167.2 2.4 collective-permute-done
  169.6 32.3 %all-gather.4.cloned.1.call-done = bf16[1,256,3072]{2,1,0:T(8,128)(2,1)} async-done(((bf16[1,16,3072]{2,1,0:T(8,128)(2,1)}), bf16[1,256,3072]{2,1,0:T(8,128)(2,1)}) %all-gather.4.cloned.1.call-update) | async-done | bytes 1572880 | tf_op jit(solution)/shard_map/all_gather | solution.py:84
  201.9 4.5 %gather_fusion.3 = bf16[128,3072]{1,0:T(8,128)(2,1)} fusion(bf16[256,3072]{1,0:T(8,128)(2,1)} %bitcast.104, s32[1024]{0:T(1024)} %pad_clamp_fusion.1), kind=kCustom, calls=%fused_computation.3 | custom fusion | bytes 1573376 | tf_op jit(solution)/shard_map/gather | solution.py:102
  206.3 2.3 fusion.3
  208.7 1.9 gather_fusion.4
  210.6 1.3 fusion.7
  211.9 24.9 %psum.15 = f32[256]{0:T(256)S(1)} all-reduce(f32[256]{0:T(256)S(1)} %fusion.7), channel_id=1, replica_groups=mesh['section'=32,'et'=16] {'et'}, use_global_device_ids=true, to_apply=%region_22.23 | all-reduce | flops 256 | bytes 2048 | tf_op jit(solution)/shard_map/psum | solution.py:107
  236.9 1.2 fusion.16
  239.2 2.8 %collective-permute-start.16 = (bf16[16,3072]{1,0:T(8,128)(2,1)S(1)}, bf16[16,3072]{1,0:T(8,128)(2,1)S(1)}, u32[]{:S(2)}, u32[]{:S(2)}) collective-permute-start(bf16[16,3072]{1,0:T(8,128)(2,1)S(1)} %fusion.20), channel_id=1, source_target_pairs={{16,0},{32,16},{48,32},{64,48},{80,64},{96,80},{112,96},{128,112},... | collective-permute-start | bytes 294920 | tf_op jit(solution)/shard_map/ppermute | solution.py:23
  241.9 1.9 fusion.9
  243.8 4.0 %collective-permute-done.16 = bf16[16,3072]{1,0:T(8,128)(2,1)S(1)} collective-permute-done((bf16[16,3072]{1,0:T(8,128)(2,1)S(1)}, bf16[16,3072]{1,0:T(8,128)(2,1)S(1)}, u32[]{:S(2)}, u32[]{:S(2)}) %collective-permute-start.16) | collective-permute-done | bytes 98336 | tf_op jit(solution)/shard_map/ppermute | solution.py:23
  247.8 1.5 copy.19
  (110 shorter events, 25.4 us)
Async XLA Ops:
  7.2 30.1 %copy-start = (bf16[1,512,3072]{2,1,0:T(8,128)(2,1)S(1)}, bf16[1,512,3072]{2,1,0:T(8,128)(2,1)}, u32[]{:S(2)}) copy-start(bf16[1,512,3072]{2,1,0:T(8,128)(2,1)} %param.19) | copy-start | bytes 9437188
  7.2 150.4 %all-reduce.2.cloned.1.call-start = ((), (), s32[]{:S(2)}) async-start(), calls=%async_computation | async-start | bytes 1572864 | tf_op jit(solution)/shard_map/psum | solution.py:93
  34.0 4.8 %copy-start.2 = (bf16[1,16,3072]{2,1,0:T(8,128)(2,1)S(1)}, bf16[1,16,3072]{2,1,0:T(8,128)(2,1)}, u32[]{:S(2)}) copy-start(bf16[1,16,3072]{2,1,0:T(8,128)(2,1)} %param.13) | copy-start | bytes 294916
  35.9 7.1 %copy-start.4 = (s32[1,256,2]{1,2,0:T(2,128)S(1)}, s32[1,256,2]{1,2,0:T(2,128)}, u32[]{:S(2)}) copy-start(s32[1,256,2]{1,2,0:T(2,128)} %param.15) | copy-start | bytes 6148
  38.8 123.5 %copy-start.1 = (bf16[1,16,3072]{2,1,0:T(8,128)(2,1)S(1)}, bf16[1,16,3072]{2,1,0:T(8,128)(2,1)}, u32[]{:S(2)}) copy-start(bf16[1,16,3072]{2,1,0:T(8,128)(2,1)} %param.10) | copy-start | bytes 294916
  38.8 163.1 %all-gather.4.cloned.1.call-start = ((), (), s32[]{:S(2)}) async-start(), calls=%async_computation.1 | async-start | bytes 1671168 | tf_op jit(solution)/shard_map/all_gather | solution.py:84
  39.0 16.0 %copy-start.10 = (f32[16]{0:T(128)}, f32[16]{0:T(128)S(1)}, u32[]{:S(2)}) copy-start(f32[16]{0:T(128)S(1)} %add_rsqrt_fusion) | copy-start | bytes 196
  40.0 10.8 %collective-permute-start.1 = (bf16[16,8]{0,1:T(8,128)(2,1)S(1)}, bf16[16,8]{0,1:T(8,128)(2,1)S(1)}, u32[]{:S(2)}, u32[]{:S(2)}) collective-permute-start(bf16[16,8]{0,1:T(8,128)(2,1)S(1)} %convolution_convert_fusion), channel_id=1, source_target_pairs={{0,1},{1,2},{2,3},{3,4},{4,5},{5,6},{6,7},{7,8},{8,9},{9,10},{10,1... | collective-permute-start | bytes 776 | tf_op jit(solution)/shard_map/ppermute | solution.py:13
  40.4 11.1 %collective-permute-start.9 = (bf16[16,8]{0,1:T(8,128)(2,1)S(1)}, bf16[16,8]{0,1:T(8,128)(2,1)S(1)}, u32[]{:S(2)}, u32[]{:S(2)}) collective-permute-start(bf16[16,8]{0,1:T(8,128)(2,1)S(1)} %convolution_convert_fusion), channel_id=1, source_target_pairs={{0,15},{1,0},{2,1},{3,2},{4,3},{5,4},{6,5},{7,6},{8,7},{9,8},{10,9... | collective-permute-start | bytes 776 | tf_op jit(solution)/shard_map/ppermute | solution.py:15
  43.0 114.5 %copy-start.5 = (f32[256]{0:T(256)}, f32[256]{0:T(256)S(1)}, u32[]{:S(2)}) copy-start(f32[256]{0:T(256)S(1)} %convert_reduce_fusion.4) | copy-start | bytes 3076
  50.8 4.2 %collective-permute-start.2 = (bf16[16,8]{0,1:T(8,128)(2,1)S(1)}, bf16[16,8]{0,1:T(8,128)(2,1)S(1)}, u32[]{:S(2)}, u32[]{:S(2)}) collective-permute-start(bf16[16,8]{0,1:T(8,128)(2,1)S(1)} %collective-permute-done.1), channel_id=1, source_target_pairs={{0,1},{1,2},{2,3},{3,4},{4,5},{5,6},{6,7},{7,8},{8,9},{9,10},{10,1... | collective-permute-start | bytes 776 | tf_op jit(solution)/shard_map/ppermute | solution.py:13
  51.4 4.3 %collective-permute-start.10 = (bf16[16,8]{0,1:T(8,128)(2,1)S(1)}, bf16[16,8]{0,1:T(8,128)(2,1)S(1)}, u32[]{:S(2)}, u32[]{:S(2)}) collective-permute-start(bf16[16,8]{0,1:T(8,128)(2,1)S(1)} %collective-permute-done.9), channel_id=1, source_target_pairs={{0,15},{1,0},{2,1},{3,2},{4,3},{5,4},{6,5},{7,6},{8,7},{9,8},{10,9... | collective-permute-start | bytes 776 | tf_op jit(solution)/shard_map/ppermute | solution.py:15
  55.0 4.2 %collective-permute-start.3 = (bf16[16,8]{0,1:T(8,128)(2,1)S(1)}, bf16[16,8]{0,1:T(8,128)(2,1)S(1)}, u32[]{:S(2)}, u32[]{:S(2)}) collective-permute-start(bf16[16,8]{0,1:T(8,128)(2,1)S(1)} %collective-permute-done.2), channel_id=1, source_target_pairs={{0,1},{1,2},{2,3},{3,4},{4,5},{5,6},{6,7},{7,8},{8,9},{9,10},{10,1... | collective-permute-start | bytes 776 | tf_op jit(solution)/shard_map/ppermute | solution.py:13
  55.7 4.2 %collective-permute-start.11 = (bf16[16,8]{0,1:T(8,128)(2,1)S(1)}, bf16[16,8]{0,1:T(8,128)(2,1)S(1)}, u32[]{:S(2)}, u32[]{:S(2)}) collective-permute-start(bf16[16,8]{0,1:T(8,128)(2,1)S(1)} %collective-permute-done.10), channel_id=1, source_target_pairs={{0,15},{1,0},{2,1},{3,2},{4,3},{5,4},{6,5},{7,6},{8,7},{9,8},{10,9... | collective-permute-start | bytes 776 | tf_op jit(solution)/shard_map/ppermute | solution.py:15
  59.2 4.2 %collective-permute-start.4 = (bf16[16,8]{0,1:T(8,128)(2,1)S(1)}, bf16[16,8]{0,1:T(8,128)(2,1)S(1)}, u32[]{:S(2)}, u32[]{:S(2)}) collective-permute-start(bf16[16,8]{0,1:T(8,128)(2,1)S(1)} %collective-permute-done.3), channel_id=1, source_target_pairs={{0,1},{1,2},{2,3},{3,4},{4,5},{5,6},{6,7},{7,8},{8,9},{9,10},{10,1... | collective-permute-start | bytes 776 | tf_op jit(solution)/shard_map/ppermute | solution.py:13
  59.9 4.2 %collective-permute-start.12 = (bf16[16,8]{0,1:T(8,128)(2,1)S(1)}, bf16[16,8]{0,1:T(8,128)(2,1)S(1)}, u32[]{:S(2)}, u32[]{:S(2)}) collective-permute-start(bf16[16,8]{0,1:T(8,128)(2,1)S(1)} %collective-permute-done.11), channel_id=1, source_target_pairs={{0,15},{1,0},{2,1},{3,2},{4,3},{5,4},{6,5},{7,6},{8,7},{9,8},{10,9... | collective-permute-start | bytes 776 | tf_op jit(solution)/shard_map/ppermute | solution.py:15
  63.5 4.2 %collective-permute-start.5 = (bf16[16,8]{0,1:T(8,128)(2,1)S(1)}, bf16[16,8]{0,1:T(8,128)(2,1)S(1)}, u32[]{:S(2)}, u32[]{:S(2)}) collective-permute-start(bf16[16,8]{0,1:T(8,128)(2,1)S(1)} %collective-permute-done.4), channel_id=1, source_target_pairs={{0,1},{1,2},{2,3},{3,4},{4,5},{5,6},{6,7},{7,8},{8,9},{9,10},{10,1... | collective-permute-start | bytes 776 | tf_op jit(solution)/shard_map/ppermute | solution.py:13
  64.1 4.2 %collective-permute-start.13 = (bf16[16,8]{0,1:T(8,128)(2,1)S(1)}, bf16[16,8]{0,1:T(8,128)(2,1)S(1)}, u32[]{:S(2)}, u32[]{:S(2)}) collective-permute-start(bf16[16,8]{0,1:T(8,128)(2,1)S(1)} %collective-permute-done.12), channel_id=1, source_target_pairs={{0,15},{1,0},{2,1},{3,2},{4,3},{5,4},{6,5},{7,6},{8,7},{9,8},{10,9... | collective-permute-start | bytes 776 | tf_op jit(solution)/shard_map/ppermute | solution.py:15
  67.7 4.2 %collective-permute-start.6 = (bf16[16,8]{0,1:T(8,128)(2,1)S(1)}, bf16[16,8]{0,1:T(8,128)(2,1)S(1)}, u32[]{:S(2)}, u32[]{:S(2)}) collective-permute-start(bf16[16,8]{0,1:T(8,128)(2,1)S(1)} %collective-permute-done.5), channel_id=1, source_target_pairs={{0,1},{1,2},{2,3},{3,4},{4,5},{5,6},{6,7},{7,8},{8,9},{9,10},{10,1... | collective-permute-start | bytes 776 | tf_op jit(solution)/shard_map/ppermute | solution.py:13
  68.4 4.2 %collective-permute-start.14 = (bf16[16,8]{0,1:T(8,128)(2,1)S(1)}, bf16[16,8]{0,1:T(8,128)(2,1)S(1)}, u32[]{:S(2)}, u32[]{:S(2)}) collective-permute-start(bf16[16,8]{0,1:T(8,128)(2,1)S(1)} %collective-permute-done.13), channel_id=1, source_target_pairs={{0,15},{1,0},{2,1},{3,2},{4,3},{5,4},{6,5},{7,6},{8,7},{9,8},{10,9... | collective-permute-start | bytes 776 | tf_op jit(solution)/shard_map/ppermute | solution.py:15
  71.9 4.2 %collective-permute-start.7 = (bf16[16,8]{0,1:T(8,128)(2,1)S(1)}, bf16[16,8]{0,1:T(8,128)(2,1)S(1)}, u32[]{:S(2)}, u32[]{:S(2)}) collective-permute-start(bf16[16,8]{0,1:T(8,128)(2,1)S(1)} %collective-permute-done.6), channel_id=1, source_target_pairs={{0,1},{1,2},{2,3},{3,4},{4,5},{5,6},{6,7},{7,8},{8,9},{9,10},{10,1... | collective-permute-start | bytes 776 | tf_op jit(solution)/shard_map/ppermute | solution.py:13
  72.6 4.2 %collective-permute-start.15 = (bf16[16,8]{0,1:T(8,128)(2,1)S(1)}, bf16[16,8]{0,1:T(8,128)(2,1)S(1)}, u32[]{:S(2)}, u32[]{:S(2)}) collective-permute-start(bf16[16,8]{0,1:T(8,128)(2,1)S(1)} %collective-permute-done.14), channel_id=1, source_target_pairs={{0,15},{1,0},{2,1},{3,2},{4,3},{5,4},{6,5},{7,6},{8,7},{9,8},{10,9... | collective-permute-start | bytes 776 | tf_op jit(solution)/shard_map/ppermute | solution.py:15
  76.1 4.2 %collective-permute-start.8 = (bf16[16,8]{0,1:T(8,128)(2,1)S(1)}, bf16[16,8]{0,1:T(8,128)(2,1)S(1)}, u32[]{:S(2)}, u32[]{:S(2)}) collective-permute-start(bf16[16,8]{0,1:T(8,128)(2,1)S(1)} %collective-permute-done.7), channel_id=1, source_target_pairs={{0,1},{1,2},{2,3},{3,4},{4,5},{5,6},{6,7},{7,8},{8,9},{9,10},{10,1... | collective-permute-start | bytes 776 | tf_op jit(solution)/shard_map/ppermute | solution.py:13
  163.0 6.6 %collective-permute-start = (bf16[16,3072]{1,0:T(8,128)(2,1)S(1)}, bf16[16,3072]{1,0:T(8,128)(2,1)}, u32[]{:S(2)}, u32[]{:S(2)}) collective-permute-start(bf16[16,3072]{1,0:T(8,128)(2,1)S(1)} %fusion.22), channel_id=1, source_target_pairs={{0,16},{16,32},{32,48},{48,64},{64,80},{80,96},{96,112},{112,128},... | collective-permute-start | bytes 294920 | tf_op jit(solution)/shard_map/ppermute | solution.py:23
  208.7 1.9 copy-start.9
  208.7 28.2 %copy-start.6 = (f32[256]{0:T(256)S(1)}, f32[256]{0:T(256)}, u32[]{:S(2)}) copy-start(f32[256]{0:T(256)} %copy-done.5) | copy-start | bytes 3076
  208.7 28.2 %copy-start.3 = (f32[3072,1]{0,1:T(1,128)S(1)}, f32[3072,1]{0,1:T(1,128)}, u32[]{:S(2)}) copy-start(f32[3072,1]{0,1:T(1,128)} %slice_convert_fusion) | copy-start | bytes 36868
  208.7 28.2 %copy-start.8 = (pred[256,8]{0,1:T(8,128)(4,1)S(1)}, pred[256,8]{0,1:T(8,128)(4,1)}, u32[]{:S(2)}) copy-start(pred[256,8]{0,1:T(8,128)(4,1)} %iota_compare_fusion) | copy-start | bytes 6148
  208.7 33.2 %copy-start.7 = (f32[256,1]{0,1:T(1,128)S(1)}, f32[256,1]{0,1:T(1,128)}, u32[]{:S(2)}) copy-start(f32[256,1]{0,1:T(1,128)} %get-tuple-element.14) | copy-start | bytes 3076
  239.2 8.6 %collective-permute-start.16 = (bf16[16,3072]{1,0:T(8,128)(2,1)S(1)}, bf16[16,3072]{1,0:T(8,128)(2,1)S(1)}, u32[]{:S(2)}, u32[]{:S(2)}) collective-permute-start(bf16[16,3072]{1,0:T(8,128)(2,1)S(1)} %fusion.20), channel_id=1, source_target_pairs={{16,0},{32,16},{48,32},{64,48},{80,64},{96,80},{112,96},{128,112},... | collective-permute-start | bytes 294920 | tf_op jit(solution)/shard_map/ppermute | solution.py:23
Sparse Core Ops, SparseCore 0:
  38.9 118.5 all-reduce.1
  159.7 42.1 all-gather.3
